TPU v7x, 256 devices: a whole 4x4x8 slice. The times are simulated.
256 devices in a mesh: segment: 4 (over x), dp: 64 (over z, y, core).
Axes of the slice: x: 4, y: 4, z: 8, core: 2. Of those that a mesh axis runs over, the one named last changes fastest.
Arguments:
- x_saved: bfloat16 [4, 8192, 1536], P('segment', 'dp'), may hold values from -6 to 6
- gains: float32 [4, 1536], P('segment'), may hold values from 0.1 to 1.9
- w_in: bfloat16 [4, 1536, 3072], P('segment', 'dp'), may hold values from -0.15625 to 0.15625
- w_out: bfloat16 [4, 3072, 1536], P('segment', None, 'dp'), may hold values from -0.109375 to 0.109375
- cotangent: bfloat16 [8192, 1536], P('dp'), may hold values from -6 to 6
- lengths: int32 [64], replicated, may hold values from 1 to 256, 8192 in all
Outputs:
- grads: bfloat16 [4, 8192, 1536], P('segment', 'dp')
- gain_grads: float32 [4, 1536], P('segment')
All inputs are finite; a program needn't handle non-finite values.
Results may differ from a plain program's by a relative error of at most 0.0075.
Values may be sent and summed in bfloat16 or wider, within the bound.
No kernel may reach another device: no remote copies, remote signals or barrier semaphores. Data moves between devices by JAX's collectives and lax.ppermute only.
A program may use at most 128 MiB of HBM per device.

v0:
```python
import jax
import jax.numpy as jnp
from jax import lax
import numpy as np
from jax.sharding import Mesh, PartitionSpec as P

DP = ("z", "y", "core")


def passed_along(x, axis, by):
    length = lax.axis_size(axis)
    pairs = [(i, i + by) for i in range(length) if 0 <= i + by < length]
    return lax.ppermute(x, axis, pairs)


def on_device(x_saved, gains, w_in, w_out, cotangent, lengths):
    rows = cotangent.shape[0]
    width = cotangent.shape[1]
    ends = jnp.cumsum(lengths)
    position = lax.axis_index(DP) * rows + jnp.arange(rows, dtype=jnp.int32)
    utter_hit = (position[:, None] >= ends[None, :]).astype(jnp.int32)
    utter = jnp.sum(utter_hit, 1)
    onehot = (utter[:, None] == jnp.arange(lengths.shape[0], dtype=jnp.int32)[None, :]).astype(
        jnp.int32
    )
    tok_len = jnp.sum(onehot * lengths[None, :], 1).astype(jnp.float32)
    weight = 2.0 * rows / (tok_len + rows)
    current = (cotangent.astype(jnp.float32) * weight[:, None]).astype(jnp.bfloat16)
    xf = x_saved[0].astype(jnp.float32)
    centered_input = xf - jnp.mean(xf, -1, keepdims=True)
    variance = jnp.mean(centered_input * centered_input, -1, keepdims=True)
    inverse_deviation = lax.rsqrt(variance + 1e-05)
    standardized_input = centered_input * inverse_deviation
    gain_vector = gains[0]
    normalized_input = (standardized_input * gain_vector).astype(jnp.bfloat16)
    w_first, w_second = (
        lax.all_gather(w_in[0], DP, axis=0, tiled=True),
        lax.all_gather(w_out[0], DP, axis=1, tiled=True),
    )

    def project_all(normed_rows, grad_in):
        hidden = jnp.dot(normed_rows, w_first, preferred_element_type=jnp.float32)
        up_grad = jnp.dot(grad_in, w_second.T, preferred_element_type=jnp.float32)
        sig = jax.nn.sigmoid(hidden)
        hid_grad = (0.5 * up_grad * (sig + hidden * sig * (1.0 - sig))).astype(jnp.bfloat16)
        return jnp.dot(hid_grad, w_first.T, preferred_element_type=jnp.float32)

    def block_back():

        def run(grad_in):
            norm_gradient = project_all(normalized_input, grad_in)
            gain_partial = jnp.sum(norm_gradient * standardized_input, 0)
            gain_scaled = norm_gradient * gain_vector
            backward_result = inverse_deviation * (
                gain_scaled
                - jnp.mean(gain_scaled, -1, keepdims=True)
                - standardized_input * jnp.mean(gain_scaled * standardized_input, -1, keepdims=True)
            )
            return (
                (grad_in.astype(jnp.float32) + backward_result).astype(jnp.bfloat16),
                gain_partial,
            )

        return run

    def pass_through(grad_in):
        return (grad_in, jnp.zeros((width,), jnp.float32))

    segments = lax.axis_size("segment")
    my_segment = lax.axis_index("segment")
    gain_local = jnp.zeros((width,), jnp.float32)
    result = current
    for level in range(segments - 1, -1, -1):
        mine = my_segment == level
        updated, gain_partial = lax.cond(mine, block_back(), pass_through, current)
        result = jnp.where(mine, updated, result)
        gain_local = jnp.where(mine, gain_partial, gain_local)
        if level > 0:
            current = passed_along(updated, "segment", -1)
    gain_total = lax.psum(lax.psum(lax.psum(gain_local, "core"), "y"), "z")
    return (result[None], gain_total[None])


def solution(mesh):
    n_seg, n_dp = mesh.devices.shape
    sizes = dict(zip(("z", "y", "core"), (n_dp // 8, 4, 2)))
    mesh = Mesh(
        np.asarray(mesh.devices).reshape(n_seg, sizes["z"], sizes["y"], sizes["core"]),
        ("segment",) + DP,
    )
    in_specs = (
        P("segment", DP, None),
        P("segment", None),
        P("segment", DP, None),
        P("segment", None, DP),
        P(DP, None),
        P(),
    )
    out_specs = (P("segment", DP, None), P("segment", None))
    return jax.shard_map(
        on_device, mesh=mesh, in_specs=in_specs, out_specs=out_specs, check_vma=False
    )
```

profile of v0, /device:TPU:8, one launch (start us, length us, event | category | flops | bytes accessed | tf_op | source)
XLA Modules:
  0.0 332.8 jit_solution(8786208565369843301)
XLA Ops:
  7.2 0.0 all-gather.7.cloned.1.call-start
  7.2 0.7 all-gather.7.cloned.1.call-update
  7.9 0.0 all-gather.5.cloned.1.call-start
  7.9 0.7 all-gather.5.cloned.1.call-update
  8.7 0.7 copy.17
  9.4 0.1 reduce-window.8
  9.5 0.1 reduce.5
  9.6 0.7 reduce.6
  10.4 0.1 convert_reduce_fusion.1
  10.4 0.7 select_reduce_fusion
  11.2 0.0 copy-start
  11.2 1.1 convert_reduce_fusion
  12.3 1.2 fusion.23
  13.6 0.0 copy-start.3
  13.6 1.5 fusion.21
  15.1 81.4 %all-gather.7.cloned.1.call-done = bf16[1,1536,3072]{2,1,0:T(8,128)(2,1)} async-done(((bf16[1,24,3072]{2,1,0:T(8,128)(2,1)}), bf16[1,1536,3072]{2,1,0:T(8,128)(2,1)}) %all-gather.7.cloned.1.call-update) | async-done | bytes 9437200 | tf_op jit(solution)/shard_map/all_gather | solution.py:37
  96.5 84.1 %all-gather.5.cloned.1.call-done = bf16[1,3072,1536]{1,2,0:T(8,128)(2,1)} async-done(((bf16[1,3072,24]{1,2,0:T(8,128)(2,1)}), bf16[1,3072,1536]{1,2,0:T(8,128)(2,1)}) %all-gather.5.cloned.1.call-update) | async-done | bytes 9437200 | tf_op jit(solution)/shard_map/all_gather | solution.py:38
  180.6 0.0 copy-done
  180.6 0.0 copy-done.3
  180.6 0.6 conditional.4
  180.7 0.6 broadcast.129
  181.2 1.3 collective-permute-start
  182.5 11.9 %collective-permute-done = bf16[128,1536]{1,0:T(8,128)(2,1)S(1)} collective-permute-done((bf16[128,1536]{1,0:T(8,128)(2,1)S(1)}, bf16[128,1536]{1,0:T(8,128)(2,1)S(1)}, u32[]{:S(2)}, u32[]{:S(2)}) %collective-permute-start) | collective-permute-done | bytes 393248 | tf_op jit(solution)/shard_map/ppermute | solution.py:13
  194.4 0.0 copy-start.1
  194.4 1.3 collective-permute-start.1
  195.7 11.0 %collective-permute-done.1 = bf16[128,1536]{1,0:T(8,128)(2,1)S(1)} collective-permute-done((bf16[128,1536]{1,0:T(8,128)(2,1)S(1)}, bf16[128,1536]{1,0:T(8,128)(2,1)S(1)}, u32[]{:S(2)}, u32[]{:S(2)}) %collective-permute-start.1) | collective-permute-done | bytes 393248 | tf_op jit(solution)/shard_map/ppermute | solution.py:13
  206.7 0.0 copy-done.1
  206.7 0.6 conditional.6
  206.7 0.6 broadcast.137
  207.3 1.3 collective-permute-start.2
  208.6 66.9 %collective-permute-done.2 = bf16[128,1536]{1,0:T(8,128)(2,1)S(1)} collective-permute-done((bf16[128,1536]{1,0:T(8,128)(2,1)S(1)}, bf16[128,1536]{1,0:T(8,128)(2,1)S(1)}, u32[]{:S(2)}, u32[]{:S(2)}) %collective-permute-start.2) | collective-permute-done | bytes 393248 | tf_op jit(solution)/shard_map/ppermute | solution.py:13
  275.4 20.4 %conditional.7 = (bf16[128,1536]{1,0:T(8,128)(2,1)S(1)}, f32[1536]{0:T(1024)S(1)}) conditional(s32[]{:T(128)} %convert_element_type.77, bf16[128,1536]{1,0:T(8,128)(2,1)S(1)} %collective-permute-done.2, (bf16[128,1536]{1,0:T(8,128)(2,1)S(1)}, f32[128,1]{0,1:T(1,128)}, bf16[3072,1536]{0,1:T(8,128)(2,1)}, bf16[128,1536]{1,0:T(8,128)(2,1)S(1)}, ...), branch_computations={%region_20.21_spmd, %region_21.25_spmd} | conditional | flops 3630562048 | bytes 36213296 | solution.py:75
  275.5 6.2 %fusion.28 = f32[128,3072]{1,0:T(8,128)} fusion(bf16[128,1536]{1,0:T(8,128)(2,1)S(1)} %get-tuple-element.84, bf16[1536,3072]{1,0:T(8,128)(2,1)} %get-tuple-element.85), kind=kOutput, calls=%fused_computation.69 | convolution fusion | flops 1207959552 | bytes 11403264 | tf_op jit(solution)/shard_map/cond/branch_1_fun/dot_general | solution.py:42
  281.7 0.0 copy-start.6
  281.7 12.7 %multiply_reduce_fusion.9 = (f32[1536]{0:T(1024)S(1)}, f32[128]{0:T(128)S(1)}, f32[128]{0:T(128)S(1)}, f32[128,1536]{1,0:T(8,128)}) fusion(f32[128,1536]{1,0:T(8,128)S(1)} %get-tuple-element.87, f32[1536]{0:T(1024)S(1)} %reduce.4, bf16[1536,3072]{1,0:T(8,128)(2,1)} %get-tuple-element.85, bf16[128,1536]{1,0:T(8,128)(2,1)S(1)} %get-tuple-element.81, ...), kind=kOutput, calls=%fused_computation.39 | convolution fusion | flops 2421029376 | bytes 22426624 | tf_op jit(solution)/shard_map/cond/branch_1_fun/dot_general | solution.py:46
  294.4 0.0 copy-done.6
  294.4 1.4 add_convert_fusion.3
  295.8 0.0 copy-start.2
  295.9 0.8 select_bitcast_fusion
  296.7 0.0 copy-done.2
  296.7 2.5 psum.21
  299.2 9.6 %psum.22 = f32[1536]{0:T(1024)S(1)} all-reduce(f32[1536]{0:T(1024)S(1)} %psum.21), channel_id=1, replica_groups=mesh['segment'=4,'z'=8,'y'=4,'core'=2] {'y'}, use_global_device_ids=true, to_apply=%region_26.27 | all-reduce | flops 1536 | bytes 12288 | tf_op jit(solution)/shard_map/psum | solution.py:80
  308.9 17.1 %psum.23 = f32[1,1536]{1,0:T(1,128)} all-reduce(f32[1,1536]{1,0:T(1,128)S(1)} %broadcast_in_dim.5), channel_id=1, replica_groups=mesh['segment'=4,'z'=8,'y'=4,'core'=2] {'z'}, use_global_device_ids=true, to_apply=%region_27.28 | all-reduce | flops 1536 | bytes 12288 | tf_op jit(solution)/shard_map/psum | solution.py:80
  (11 shorter events, 0.1 us)
Async XLA Ops:
  7.2 89.4 %all-gather.7.cloned.1.call-start = ((), (), s32[]{:S(2)}) async-start(), calls=%async_computation.1 | async-start | bytes 9584640 | tf_op jit(solution)/shard_map/all_gather | solution.py:37
  7.9 172.7 %all-gather.5.cloned.1.call-start = ((), (), s32[]{:S(2)}) async-start(), calls=%async_computation | async-start | bytes 9584640 | tf_op jit(solution)/shard_map/all_gather | solution.py:38
  11.2 169.4 %copy-start = (f32[1,1536]{1,0:T(1,128)S(1)}, f32[1,1536]{1,0:T(1,128)}, u32[]{:S(2)}) copy-start(f32[1,1536]{1,0:T(1,128)} %param.15) | copy-start | bytes 18436
  13.6 167.0 %copy-start.3 = (f32[128,1]{0,1:T(1,128)}, f32[128,1]{0,1:T(1,128)S(1)}, u32[]{:S(2)}) copy-start(f32[128,1]{0,1:T(1,128)S(1)} %get-tuple-element.189) | copy-start | bytes 1540
  181.2 13.2 %collective-permute-start = (bf16[128,1536]{1,0:T(8,128)(2,1)S(1)}, bf16[128,1536]{1,0:T(8,128)(2,1)S(1)}, u32[]{:S(2)}, u32[]{:S(2)}) collective-permute-start(bf16[128,1536]{1,0:T(8,128)(2,1)S(1)} %get-tuple-element.98), channel_id=1, source_target_pairs={{64,0},{128,64},{192,128},{65,1},{129,65},{193,129},{66,2},{130,66... | collective-permute-start | bytes 1179656 | tf_op jit(solution)/shard_map/ppermute | solution.py:13
  194.4 12.3 %copy-start.1 = (f32[1536]{0:T(1024)}, f32[1536]{0:T(1024)S(1)}, u32[]{:S(2)}) copy-start(f32[1536]{0:T(1024)S(1)} %get-tuple-element.104) | copy-start | bytes 18436
  194.4 12.3 %collective-permute-start.1 = (bf16[128,1536]{1,0:T(8,128)(2,1)S(1)}, bf16[128,1536]{1,0:T(8,128)(2,1)S(1)}, u32[]{:S(2)}, u32[]{:S(2)}) collective-permute-start(bf16[128,1536]{1,0:T(8,128)(2,1)S(1)} %get-tuple-element.99), channel_id=1, source_target_pairs={{64,0},{128,64},{192,128},{65,1},{129,65},{193,129},{66,2},{130,66... | collective-permute-start | bytes 1179656 | tf_op jit(solution)/shard_map/ppermute | solution.py:13
  207.3 68.2 %collective-permute-start.2 = (bf16[128,1536]{1,0:T(8,128)(2,1)S(1)}, bf16[128,1536]{1,0:T(8,128)(2,1)S(1)}, u32[]{:S(2)}, u32[]{:S(2)}) collective-permute-start(bf16[128,1536]{1,0:T(8,128)(2,1)S(1)} %get-tuple-element.100), channel_id=1, source_target_pairs={{64,0},{128,64},{192,128},{65,1},{129,65},{193,129},{66,2},{130,66... | collective-permute-start | bytes 1179656 | tf_op jit(solution)/shard_map/ppermute | solution.py:13
  281.7 12.7 %copy-start.6 = (f32[128,1]{0,1:T(1,128)S(1)}, f32[128,1]{0,1:T(1,128)}, u32[]{:S(2)}) copy-start(f32[128,1]{0,1:T(1,128)} %get-tuple-element.82) | copy-start | bytes 1540 | tf_op jit(solution)/shard_map/cond
  295.8 0.8 copy-start.2
Sparse Core Ops, SparseCore 0:
  10.7 85.7 all-gather.6
  99.3 81.3 all-gather.4
where the time goes:
time: 333 us
  waiting for transfers between devices  257 us (77%)
  blocking collectives  29.2 us (9%)
  matrix products  18.9 us (6%)
  between operations  14.2 us (4%)
  other arithmetic  7.94 us (2%)
  starting transfers between devices  3.92 us (1%)
    ppermute x3, waiting for transfers between devices, passed_along(): return lax.ppermute(x, axis, pairs)  89.7 us
    all_gather x1, waiting for transfers between devices, on_device(): lax.all_gather(w_out[0], DP, axis=1, tiled=True)  84.1 us
    all_gather x1, waiting for transfers between devices, on_device(): lax.all_gather(w_in[0], DP, axis=0, tiled=True)  81.4 us
    psum x3, blocking collectives, on_device(): gain_total = lax.psum(lax.psum(lax.psum(gain_local, 'core'), 'y'), 'z')  29.2 us
    dot_general x1, matrix products, project_all(): return jnp.dot(hid_grad, w_first.T, preferred_element_type=jnp.float32)  12.7 us
  transfers between devices with their start and end apart: 5, of which 5 were waited for; matrix products, arithmetic and copies ran while one was open for 2% of the time, Pallas kernels for 0%

commit v1 on v0

--- a/solution.py
+++ b/solution.py
@@ -3,6 +3,7 @@
 from jax import lax
 import numpy as np
 from jax.sharding import Mesh, PartitionSpec as P
+from jax.lax import all_to_all, axis_size
 
 DP = ("z", "y", "core")
 
@@ -35,7 +36,7 @@
     normalized_input = (standardized_input * gain_vector).astype(jnp.bfloat16)
     w_first, w_second = (
         lax.all_gather(w_in[0], DP, axis=0, tiled=True),
-        lax.all_gather(w_out[0], DP, axis=1, tiled=True),
+        jnp.concatenate(all_to_all(jnp.stack(axis_size(DP) * [w_out[0]]), DP, 0, 0), axis=1),
     )
 
     def project_all(normed_rows, grad_in):

time: 333 us -> 413 us (1.24)
  waiting for transfers between devices: 257 us -> 319 us
  starting transfers between devices: 3.92 us -> 16.3 us
  blocking collectives: 29.2 us -> 34.8 us
  other arithmetic: 7.94 us -> 3.47 us
    all_to_all x0 -> x1, waiting for transfers between devices: none -> 234 us  [on_device(): all_to_all(jnp.stack(axis_size(DP) * [w_out[0]]), DP, 0, 0)]
    all_gather x1 -> x0, waiting for transfers between devices: 84.1 us -> none  [on_device(): lax.all_gather(w_out[0], DP, axis=1, tiled=True)]
    all_gather x1, waiting for transfers between devices: 81.4 us -> 0.01 us  [on_device(): lax.all_gather(w_in[0], DP, axis=0, tiled=True)]
    all_to_all x0 -> x1, starting transfers between devices: none -> 12.4 us  [on_device(): all_to_all(jnp.stack(axis_size(DP) * [w_out[0]]), DP, 0, 0)]
    ppermute x3, waiting for transfers between devices: 89.7 us -> 83.8 us  [passed_along(): return lax.ppermute(x, axis, pairs)]
    psum x3, blocking collectives: 29.2 us -> 34.8 us  [on_device(): gain_total = lax.psum(lax.psum(lax.psum(gain_local, 'core'), 'y'), 'z')]
  transfers between devices with their start and end apart: 5 -> 5, of which waited for: 5 -> 4; matrix products, arithmetic and copies ran while one was open for 2% -> 0% of each run, Pallas kernels for 0% -> 0%
where the time goes in v1:
time: 413 us; the launch traced here: 412 us
  waiting for transfers between devices  319 us (77%)
  blocking collectives  34.8 us (8%)
  matrix products  18.9 us (5%)
  starting transfers between devices  16.3 us (4%)
  between operations  14.2 us (3%)
  local copies, waits for them, and re-layouts  5.97 us (1%)
    all_to_all x1, waiting for transfers between devices, on_device(): all_to_all(jnp.stack(axis_size(DP) * [w_out[0]]), DP, 0, 0)  234 us
    ppermute x3, waiting for transfers between devices, passed_along(): return lax.ppermute(x, axis, pairs)  83.8 us
    psum x3, blocking collectives, on_device(): gain_total = lax.psum(lax.psum(lax.psum(gain_local, 'core'), 'y'), 'z')  34.8 us
    dot_general x1, matrix products, project_all(): return jnp.dot(hid_grad, w_first.T, preferred_element_type=jnp.float32)  12.7 us
    all_to_all x1, starting transfers between devices, on_device(): all_to_all(jnp.stack(axis_size(DP) * [w_out[0]]), DP, 0, 0)  12.4 us
  transfers between devices with their start and end apart: 5, of which 4 were waited for; matrix products, arithmetic and copies ran while one was open for 0% of the time, Pallas kernels for 0%

profile of v1, /device:TPU:8, one launch (start us, length us, event | category | flops | bytes accessed | tf_op | source)
XLA Modules:
  0.0 412.3 jit_solution(10526616846172965345)
XLA Ops:
  7.2 5.8 %stack.3 = bf16[64,3072,24]{1,2,0:T(8,128)(2,1)} broadcast(bf16[3072,24]{0,1:T(8,128)(2,1)} %bitcast.50), dimensions={1,2} | broadcast | bytes 9584640 | tf_op jit(solution)/shard_map/stack | solution.py:39
  13.0 0.0 copy-start.3
  13.0 0.0 copy-start.2
  13.0 0.0 copy-start
  13.0 0.0 copy-start.1
  13.0 12.4 %all-to-all-start = ((bf16[64,3072,24]{1,2,0:T(8,128)(2,1)}), bf16[64,3072,24]{1,2,0:T(8,128)(2,1)}, u32[]{:S(2)}, u32[]{:S(2)}) async-start(bf16[64,3072,24]{1,2,0:T(8,128)(2,1)} %stack.3), calls=%async_computation | async-start | bytes 18874368 | tf_op jit(solution)/shard_map/all_to_all | solution.py:39
  25.4 0.0 all-gather.3.cloned.1.call-start
  25.5 0.7 all-gather.3.cloned.1.call-update
  26.2 0.0 copy-done.3
  26.2 0.1 copy.15
  26.3 0.1 reduce-window.8
  26.4 0.1 reduce.5
  26.5 0.0 copy-done.2
  26.5 0.1 convert_reduce_fusion.1
  26.6 0.1 select_reduce_fusion
  26.7 0.0 copy-done
  26.7 0.1 convert_reduce_fusion
  26.9 0.3 fusion.23
  27.2 0.0 copy-done.1
  27.2 0.3 fusion.21
  27.5 234.1 %all-to-all-done = bf16[64,3072,24]{1,2,0:T(8,128)(2,1)} async-done(((bf16[64,3072,24]{1,2,0:T(8,128)(2,1)}), bf16[64,3072,24]{1,2,0:T(8,128)(2,1)}, u32[]{:S(2)}, u32[]{:S(2)}) %all-to-all-start) | async-done | bytes 9437216 | tf_op jit(solution)/shard_map/all_to_all | solution.py:39
  261.7 0.0 all-gather.3.cloned.1.call-done
  261.7 1.3 collective-permute-start
  263.0 10.1 %collective-permute-done = bf16[128,1536]{1,0:T(8,128)(2,1)S(1)} collective-permute-done((bf16[128,1536]{1,0:T(8,128)(2,1)S(1)}, bf16[128,1536]{1,0:T(8,128)(2,1)S(1)}, u32[]{:S(2)}, u32[]{:S(2)}) %collective-permute-start) | collective-permute-done | bytes 393248 | tf_op jit(solution)/shard_map/ppermute | solution.py:14
  273.1 1.3 collective-permute-start.1
  274.4 9.2 %collective-permute-done.1 = bf16[128,1536]{1,0:T(8,128)(2,1)S(1)} collective-permute-done((bf16[128,1536]{1,0:T(8,128)(2,1)S(1)}, bf16[128,1536]{1,0:T(8,128)(2,1)S(1)}, u32[]{:S(2)}, u32[]{:S(2)}) %collective-permute-start.1) | collective-permute-done | bytes 393248 | tf_op jit(solution)/shard_map/ppermute | solution.py:14
  283.6 1.3 collective-permute-start.2
  284.9 64.5 %collective-permute-done.2 = bf16[128,1536]{1,0:T(8,128)(2,1)S(1)} collective-permute-done((bf16[128,1536]{1,0:T(8,128)(2,1)S(1)}, bf16[128,1536]{1,0:T(8,128)(2,1)S(1)}, u32[]{:S(2)}, u32[]{:S(2)}) %collective-permute-start.2) | collective-permute-done | bytes 393248 | tf_op jit(solution)/shard_map/ppermute | solution.py:14
  349.4 20.4 %conditional.7 = (bf16[128,1536]{1,0:T(8,128)(2,1)S(1)}, f32[1536]{0:T(1024)S(1)}) conditional(s32[]{:T(128)} %convert_element_type.77, bf16[128,1536]{1,0:T(8,128)(2,1)S(1)} %collective-permute-done.2, (bf16[128,1536]{1,0:T(8,128)(2,1)S(1)}, f32[128,1]{0,1:T(1,128)S(1)}, bf16[3072,1536]{0,1:T(8,128)(2,1)}, bf16[128,1536]{1,0:T(8,128)(2,1)S(1)}, ...), branch_computations={%region_20.21_spmd, %region_21.25_spmd} | conditional | flops 3630562048 | bytes 36211220 | solution.py:76
  349.4 6.2 %fusion.28 = f32[128,3072]{1,0:T(8,128)} fusion(bf16[128,1536]{1,0:T(8,128)(2,1)S(1)} %get-tuple-element.84, bf16[1536,3072]{1,0:T(8,128)(2,1)} %get-tuple-element.85), kind=kOutput, calls=%fused_computation.69 | convolution fusion | flops 1207959552 | bytes 11403264 | tf_op jit(solution)/shard_map/cond/branch_1_fun/dot_general | solution.py:43
  355.7 12.7 %multiply_reduce_fusion.9 = (f32[1536]{0:T(1024)S(1)}, f32[128]{0:T(128)S(1)}, f32[128]{0:T(128)S(1)}, f32[128,1536]{1,0:T(8,128)}) fusion(f32[128,1536]{1,0:T(8,128)S(1)} %get-tuple-element.87, f32[1536]{0:T(1024)S(1)} %reduce.4, bf16[1536,3072]{1,0:T(8,128)(2,1)} %get-tuple-element.85, bf16[128,1536]{1,0:T(8,128)(2,1)S(1)} %get-tuple-element.81, ...), kind=kOutput, calls=%fused_computation.39 | convolution fusion | flops 2421029376 | bytes 22426624 | tf_op jit(solution)/shard_map/cond/branch_1_fun/dot_general | solution.py:47
  368.4 1.4 add_convert_fusion.3
  369.8 2.5 psum.21
  372.3 11.6 %psum.22 = f32[1536]{0:T(1024)S(1)} all-reduce(f32[1536]{0:T(1024)S(1)} %psum.21), channel_id=1, replica_groups=mesh['segment'=4,'z'=8,'y'=4,'core'=2] {'y'}, use_global_device_ids=true, to_apply=%region_26.27 | all-reduce | flops 1536 | bytes 12288 | tf_op jit(solution)/shard_map/psum | solution.py:81
  383.9 20.7 %psum.23 = f32[1,1536]{1,0:T(1,128)} all-reduce(f32[1,1536]{1,0:T(1,128)S(1)} %broadcast_in_dim.5), channel_id=1, replica_groups=mesh['segment'=4,'z'=8,'y'=4,'core'=2] {'z'}, use_global_device_ids=true, to_apply=%region_27.28 | all-reduce | flops 1536 | bytes 12288 | tf_op jit(solution)/shard_map/psum | solution.py:81
  404.6 0.8 select_bitcast_fusion
  (16 shorter events, 0.2 us)
Async XLA Ops:
  13.0 13.2 %copy-start.3 = (s32[64]{0:T(128)S(1)}, s32[64]{0:T(128)}, u32[]{:S(2)}) copy-start(s32[64]{0:T(128)} %param.19) | copy-start | bytes 772
  13.0 13.5 %copy-start.2 = (f32[1,1536]{1,0:T(1,128)S(1)}, f32[1,1536]{1,0:T(1,128)}, u32[]{:S(2)}) copy-start(f32[1,1536]{1,0:T(1,128)} %param.15) | copy-start | bytes 18436
  13.0 13.7 %copy-start = (bf16[1,128,1536]{2,1,0:T(8,128)(2,1)S(1)}, bf16[1,128,1536]{2,1,0:T(8,128)(2,1)}, u32[]{:S(2)}) copy-start(bf16[1,128,1536]{2,1,0:T(8,128)(2,1)} %param.14) | copy-start | bytes 1179652
  13.0 14.2 %copy-start.1 = (bf16[128,1536]{1,0:T(8,128)(2,1)S(1)}, bf16[128,1536]{1,0:T(8,128)(2,1)}, u32[]{:S(2)}) copy-start(bf16[128,1536]{1,0:T(8,128)(2,1)} %param.18) | copy-start | bytes 1179652
  13.0 248.7 %all-to-all-start = ((bf16[64,3072,24]{1,2,0:T(8,128)(2,1)}), bf16[64,3072,24]{1,2,0:T(8,128)(2,1)}, u32[]{:S(2)}, u32[]{:S(2)}) async-start(bf16[64,3072,24]{1,2,0:T(8,128)(2,1)} %stack.3), calls=%async_computation | async-start | bytes 18874368 | tf_op jit(solution)/shard_map/all_to_all | solution.py:39
  25.4 236.2 %all-gather.3.cloned.1.call-start = ((), (), s32[]{:S(2)}) async-start(), calls=%async_computation.1 | async-start | bytes 9584640 | tf_op jit(solution)/shard_map/all_gather | solution.py:38
  261.7 11.4 %collective-permute-start = (bf16[128,1536]{1,0:T(8,128)(2,1)S(1)}, bf16[128,1536]{1,0:T(8,128)(2,1)S(1)}, u32[]{:S(2)}, u32[]{:S(2)}) collective-permute-start(bf16[128,1536]{1,0:T(8,128)(2,1)S(1)} %get-tuple-element.98), channel_id=1, source_target_pairs={{64,0},{128,64},{192,128},{65,1},{129,65},{193,129},{66,2},{130,66... | collective-permute-start | bytes 1179656 | tf_op jit(solution)/shard_map/ppermute | solution.py:14
  273.1 10.5 %collective-permute-start.1 = (bf16[128,1536]{1,0:T(8,128)(2,1)S(1)}, bf16[128,1536]{1,0:T(8,128)(2,1)S(1)}, u32[]{:S(2)}, u32[]{:S(2)}) collective-permute-start(bf16[128,1536]{1,0:T(8,128)(2,1)S(1)} %get-tuple-element.99), channel_id=1, source_target_pairs={{64,0},{128,64},{192,128},{65,1},{129,65},{193,129},{66,2},{130,66... | collective-permute-start | bytes 1179656 | tf_op jit(solution)/shard_map/ppermute | solution.py:14
  283.6 65.8 %collective-permute-start.2 = (bf16[128,1536]{1,0:T(8,128)(2,1)S(1)}, bf16[128,1536]{1,0:T(8,128)(2,1)S(1)}, u32[]{:S(2)}, u32[]{:S(2)}) collective-permute-start(bf16[128,1536]{1,0:T(8,128)(2,1)S(1)} %get-tuple-element.100), channel_id=1, source_target_pairs={{64,0},{128,64},{192,128},{65,1},{129,65},{193,129},{66,2},{130,66... | collective-permute-start | bytes 1179656 | tf_op jit(solution)/shard_map/ppermute | solution.py:14
Sparse Core Ops, SparseCore 0:
  29.0 151.9 all-gather.2
